TPU v7x, 512 devices: a whole 4x8x8 slice. The times are simulated.
512 devices in a mesh: req: 128 (over z, y, core), grp: 4 (over x).
Axes of the slice: x: 4, y: 8, z: 8, core: 2. Of those that a mesh axis runs over, the one named last changes fastest.
Arguments:
- owner_slab: bfloat16 [65536, 1024], P('req'), may hold values from -6 to 6
- segment_ids: int32 [128, 512], P('req'), may hold values from 0 to 511, as said below
- head_weights: bfloat16 [1024, 16, 192], P(None, 'grp')
- merge_weights: bfloat16 [16, 64, 1024], P('grp'), may hold values from -0.1875 to 0.1875
- first_gain: float32 [1024], replicated, may hold values from 0.25 to 1.75
- first_bias: float32 [1024], replicated, may hold values from -3 to 3
- up_weights: bfloat16 [1024, 4096], P('req', 'grp'), may hold values from -0.1875 to 0.1875
- down_weights: bfloat16 [4096, 1024], P('grp', 'req'), may hold values from -0.09375 to 0.09375
- second_gain: float32 [1024], replicated, may hold values from 0.25 to 1.75
- second_bias: float32 [1024], replicated, may hold values from -3 to 3
- page_table: int32 [128, 4], P('req'), may hold values from 0 to 3, each once within a row
- row_map: int32 [128, 4, 128], P('req', 'grp'), may hold values from 0 to 127, each once within a row
Outputs:
- layer_out: bfloat16 [65536, 1024], P(('req', 'grp'))
- cache_pages: bfloat16 [512, 128, 16, 128], P('req', None, 'grp')
Inputs may be any that keep to these rules, and one draw needn't show every extreme that they name: `segment_ids`: within each slab the ids start at 0, never fall and rise by at most one from row to row; in one slab all 512 rows form a single request, and in one other slab every row is a request of its own.
All inputs are finite; a program needn't handle non-finite values.
Results may differ from a plain program's by a relative error of at most 0.0075.
Values may be sent and summed in bfloat16 or wider, within the bound.
No kernel may reach another device: no remote copies, remote signals or barrier semaphores. Data moves between devices by JAX's collectives and lax.ppermute only.
A program may use at most 64 MiB of HBM per device.

v0:
```python
import math
import jax
import jax.numpy as jnp
import numpy as np
from jax import lax
from jax.sharding import Mesh
from jax.sharding import PartitionSpec as P

EPSILON = 1e-05
REQ = ("rz", "ry", "rc")


def layer_norm(values, gain, bias):
    center = values - jnp.mean(values, axis=-1, keepdims=True)
    spread = jnp.mean(center * center, axis=-1, keepdims=True)
    return center * lax.rsqrt(spread + EPSILON) * gain + bias


def split_req(mesh):
    column = mesh.devices[:, 0]
    try:
        cores = len({d.core_on_chip for d in column})
        ys = len({d.coords[1] for d in column})
        zs = len({d.coords[2] for d in column})
    except AttributeError:
        return (column.shape[0], 1, 1)
    if zs * ys * cores != column.shape[0]:
        return (column.shape[0], 1, 1)
    return (zs, ys, cores)


def gather_rows(block, first, second):
    a = lax.all_gather(block, first, axis=0, tiled=False)
    b = lax.all_gather(a, second, axis=0, tiled=False)
    c = lax.all_gather(b, "rc", axis=0, tiled=False)
    if first == "ry":
        c = jnp.transpose(c, (1, 2, 0, 3, 4))
    else:
        c = jnp.transpose(c, (2, 1, 0, 3, 4))
    return c.reshape(-1, block.shape[1])


def local(
    owner_slab,
    segment_ids,
    head_weights,
    merge_weights,
    first_gain,
    first_bias,
    up_weights,
    down_weights,
    second_gain,
    second_bias,
    page_table,
    row_map,
):
    group = lax.axis_size("grp")
    owners = lax.axis_size(REQ)
    zs = lax.axis_size("rz")
    rows_all = owner_slab.shape[0]
    width = owner_slab.shape[1]
    quarter = rows_all // group
    local_heads = head_weights.shape[1]
    head_dim = head_weights.shape[2] // 3
    up_full = gather_rows(up_weights, "ry", "rz")
    down_full_t = gather_rows(jnp.transpose(down_weights), "rz", "ry")
    projected = jnp.einsum(
        "nd,dhc->nhc", owner_slab, head_weights, preferred_element_type=jnp.float32
    ).astype(jnp.bfloat16)
    queries = jnp.moveaxis(projected[:, :, :head_dim], 1, 0)
    key_rows = jnp.moveaxis(projected[:, :, head_dim : 2 * head_dim], 1, 0)
    value_rows = jnp.moveaxis(projected[:, :, 2 * head_dim :], 1, 0)
    segment = segment_ids[0]
    position = jnp.arange(rows_all, dtype=jnp.int32)
    allowed = (position[:, None] >= position[None, :]) & (segment[:, None] == segment[None, :])
    scale = 1.0 / math.sqrt(head_dim)

    def one_head(operands):
        query_head, key_head, value_head = operands
        scores = (
            lax.dot_general(
                query_head, key_head, (((1,), (1,)), ((), ())), preferred_element_type=jnp.float32
            )
            * scale
        )
        scores = jnp.where(allowed, scores, -1e30)
        probs = jax.nn.softmax(scores, axis=-1).astype(jnp.bfloat16)
        return jnp.dot(probs, value_head, preferred_element_type=jnp.float32).astype(jnp.bfloat16)

    attended = jnp.moveaxis(lax.map(one_head, (queries, key_rows, value_rows)), 0, 1)
    own = lax.axis_index("grp")
    own_rows = lax.dynamic_slice_in_dim(owner_slab, own * quarter, quarter, 0).astype(jnp.float32)
    partial_rows = jnp.einsum(
        "nhd,hde->ne", attended, merge_weights, preferred_element_type=jnp.float32
    )
    mixed = lax.psum_scatter(partial_rows, "grp", scatter_dimension=0, tiled=True)
    hidden = layer_norm(own_rows + mixed, first_gain, first_bias).astype(jnp.bfloat16)
    slots = quarter // owners
    placed = jnp.zeros_like(hidden).at[row_map[0, 0]].set(hidden)
    staged = placed.reshape(zs, owners // zs, slots * width)
    staged = lax.all_to_all(staged, "rz", split_axis=0, concat_axis=0, tiled=True)
    staged = lax.all_to_all(staged, ("ry", "rc"), split_axis=1, concat_axis=1, tiled=True)
    even_rows = staged.reshape(quarter, width)
    group_rows = lax.all_gather(even_rows, "grp", axis=0, tiled=True)
    raised = jnp.dot(group_rows, up_full, preferred_element_type=jnp.float32)
    activated = jax.nn.gelu(raised, approximate=False).astype(jnp.bfloat16)
    lowered_all = lax.dot_general(
        activated, down_full_t, (((1,), (1,)), ((), ())), preferred_element_type=jnp.float32
    )
    lowered = lax.psum_scatter(lowered_all, "grp", scatter_dimension=0, tiled=True)
    layer_out = layer_norm(
        even_rows.astype(jnp.float32) + lowered, second_gain, second_bias
    ).astype(jnp.bfloat16)
    page_count = page_table.shape[1]
    page_rows = rows_all // page_count
    stacked = projected[:, :, head_dim:].reshape(page_count, page_rows, local_heads, 2 * head_dim)
    cache_pages = jnp.zeros_like(stacked).at[page_table[0]].set(stacked)
    return (layer_out, cache_pages)


def solution(mesh):
    zs, ys, cores = split_req(mesh)
    devices = np.asarray(mesh.devices).reshape(zs, ys, cores, mesh.devices.shape[1])
    inner = Mesh(devices, REQ + ("grp",))
    in_specs = (
        P(REQ, None),
        P(REQ, None),
        P(None, "grp", None),
        P("grp", None, None),
        P(),
        P(),
        P(REQ, "grp"),
        P("grp", REQ),
        P(),
        P(),
        P(REQ, None),
        P(REQ, "grp", None),
    )
    out_specs = (P(REQ + ("grp",), None), P(REQ, None, "grp", None))
    return jax.shard_map(local, mesh=inner, in_specs=in_specs, out_specs=out_specs, check_vma=False)
```

profile of v0, /device:TPU:1, one launch (start us, length us, event | category | flops | bytes accessed | tf_op | source)
XLA Modules:
  0.0 255.3 jit_solution(2603240170650563449)
XLA Ops:
  8.1 23.0 %all-gather = bf16[64,1024]{1,0:T(8,128)(2,1)} all-gather(bf16[8,1024]{1,0:T(8,128)(2,1)} %param.20), channel_id=2, replica_groups=mesh['rz'=8,'ry'=8,'rc'=2,'grp'=4] {'ry'}, dimensions={0}, use_global_device_ids=true | all-gather | bytes 147456 | tf_op jit(solution)/shard_map/all_gather | solution.py:33
  31.1 27.1 %all-gather.3 = bf16[64,1024]{1,0:T(8,128)(2,1)} all-gather(bf16[8,1024]{1,0:T(8,128)(2,1)} %bitcast.90), channel_id=5, replica_groups=mesh['rz'=8,'ry'=8,'rc'=2,'grp'=4] {'rz'}, dimensions={0}, use_global_device_ids=true | all-gather | bytes 147456 | tf_op jit(solution)/shard_map/all_gather | solution.py:33
  58.3 2.2 fusion.101
  60.7 0.5 copy-done.7
  61.2 3.7 %while.11 = (s32[]{:T(128)}, bf16[4,512,64]{1,2,0:T(8,128)(2,1)S(1)}, bf16[4,512,64]{1,2,0:T(8,128)(2,1)S(1)}, bf16[4,512,64]{1,2,0:T(8,128)(2,1)S(1)}, bf16[4,5...) while((s32[]{:T(128)}, bf16[4,512,64]{1,2,0:T(8,128)(2,1)S(1)}, ...), condition=%wide.region_3.4_spmd.clone, body=%wide.region_0.3_spmd.clone.sunk | while | flops 70024192 | bytes 3424341 | solution.py:90
  61.2 0.4 fusion.113
  62.1 0.4 fusion.113
  62.7 0.3 fusion.115
  63.1 0.4 fusion.113
  63.7 0.3 fusion.115
  64.0 0.4 fusion.113
  64.6 0.3 fusion.115
  64.9 2.8 %convolution_bitcast_fusion = f32[512,1024]{1,0:T(8,128)} fusion(bf16[4,64,1024]{2,1,0:T(8,128)(2,1)} %param.17, bf16[4,512,64]{1,2,0:T(8,128)(2,1)S(1)} %get-tuple-element.34), kind=kOutput, calls=%fused_computation.40 | convolution fusion | flops 268435456 | bytes 2883584 | tf_op jit(solution)/shard_map/nhd,hde->ne/dot_general | solution.py:93
  67.9 10.0 %all-gather.14.cloned.1.call-done = bf16[64,8,1024]{2,1,0:T(8,128)(2,1)} async-done(((bf16[8,8,1024]{2,1,0:T(8,128)(2,1)}), bf16[64,8,1024]{2,1,0:T(8,128)(2,1)}) %all-gather.14.cloned.1.call-update) | async-done | bytes 1048592 | tf_op jit(solution)/shard_map/all_gather | solution.py:34
  78.0 41.6 %all-gather.18.cloned.1.call-done = bf16[64,8,1024]{2,1,0:T(8,128)(2,1)} async-done(((bf16[8,8,1024]{2,1,0:T(8,128)(2,1)}), bf16[64,8,1024]{2,1,0:T(8,128)(2,1)}) %all-gather.18.cloned.1.call-update) | async-done | bytes 1048592 | tf_op jit(solution)/shard_map/all_gather | solution.py:34
  119.7 1.2 fusion.64
  120.9 1.2 multiply_reduce_fusion.1
  122.2 1.9 scatter_custom_fusion
  124.1 16.0 %all_to_all.10 = bf16[8,16,1024]{2,1,0:T(8,128)(2,1)S(1)} all-to-all(bf16[8,16,1024]{2,1,0:T(8,128)(2,1)S(1)} %bitcast.87), channel_id=1, replica_groups=mesh['rz'=8,'ry'=8,'rc'=2,'grp'=4] {'rz'}, dimensions={0} | all-to-all | bytes 524288 | tf_op jit(solution)/shard_map/all_to_all | solution.py:101
  140.3 21.8 %all_to_all.11 = bf16[8,16,1024]{2,0,1:T(8,128)(2,1)S(1)} all-to-all(bf16[8,16,1024]{2,0,1:T(8,128)(2,1)S(1)} %copy.42), channel_id=1, replica_groups=mesh['rz'=8,'ry'=8,'rc'=2,'grp'=4] {'ry','rc'}, dimensions={1} | all-to-all | bytes 524288 | tf_op jit(solution)/shard_map/all_to_all | solution.py:102
  162.1 0.9 copy.43
  163.2 3.2 %copy.44 = bf16[8,8,2,8,1024]{4,3,2,1,0:T(8,128)(2,1)} copy(bf16[8,8,2,8,1024]{4,3,1,0,2:T(8,128)(2,1)} %bitcast.80) | data formatting | bytes 4194304 | tf_op jit(solution)/shard_map/transpose | solution.py:37
  166.5 3.1 %copy.45 = bf16[8,8,2,8,1024]{4,3,2,1,0:T(8,128)(2,1)} copy(bf16[8,8,2,8,1024]{4,3,0,1,2:T(8,128)(2,1)} %bitcast.81) | data formatting | bytes 4194304 | tf_op jit(solution)/shard_map/transpose | solution.py:39
  169.6 26.6 %all-gather.12.cloned.1.call-done = bf16[512,1024]{1,0:T(8,128)(2,1)} async-done(((bf16[128,1024]{1,0:T(8,128)(2,1)}), bf16[512,1024]{1,0:T(8,128)(2,1)}) %all-gather.12.cloned.1.call-update) | async-done | bytes 1048592 | tf_op jit(solution)/shard_map/all_gather | solution.py:104
  196.3 10.1 %fusion.25 = f32[512,1024]{1,0:T(8,128)} fusion(bf16[1024,1024]{1,0:T(8,128)(2,1)} %bitcast.83, bf16[512,1024]{1,0:T(8,128)(2,1)} %all-gather.12.cloned.1.call-done, bf16[1024,1024]{1,0:T(8,128)(2,1)} %bitcast.82), kind=kOutput, calls=%fused_computation.41 | convolution fusion | flops 2181562368 | bytes 7340032 | tf_op jit(solution)/shard_map/dot_general | solution.py:107
  206.6 0.4 copy.46
  207.2 0.8 scatter_fusion
  208.0 1.2 copy.47
  209.2 34.7 %reduce-scatter.5.cloned.1.call-done = f32[128,1024]{1,0:T(8,128)} async-done(((f32[512,1024]{1,0:T(8,128)}), f32[128,1024]{1,0:T(8,128)}) %reduce-scatter.5.cloned.1.call-update) | async-done | bytes 524304 | tf_op jit(solution)/shard_map/reduce_scatter | solution.py:110
  243.9 1.2 fusion.63
  245.0 1.2 multiply_reduce_fusion
  246.3 1.9 add_convert_fusion
  (54 shorter events, 2.6 us)
Async XLA Ops:
  8.0 50.3 %copy-start = (bf16[1024,4,192]{0,2,1:T(8,128)(2,1)S(1)}, bf16[1024,4,192]{0,2,1:T(8,128)(2,1)}, u32[]{:S(2)}) copy-start(bf16[1024,4,192]{0,2,1:T(8,128)(2,1)} %param.16) | copy-start | bytes 4718596
  8.0 69.9 %all-gather.14.cloned.1.call-start = ((), (), s32[]{:S(2)}) async-start(), calls=%async_computation.7 | async-start | bytes 1179648 | tf_op jit(solution)/shard_map/all_gather | solution.py:34
  31.1 88.5 %all-gather.18.cloned.1.call-start = ((), (), s32[]{:S(2)}) async-start(), calls=%async_computation.9 | async-start | bytes 1179648 | tf_op jit(solution)/shard_map/all_gather | solution.py:34
  58.2 61.5 %reduce-scatter.3.cloned.1.call-start = ((), (), s32[]{:S(2)}) async-start(), calls=%async_computation.4 | async-start | bytes 2621440 | tf_op jit(solution)/shard_map/reduce_scatter | solution.py:96
  60.5 0.7 copy-start.7
  67.8 51.9 %copy-start.8 = (s32[1,1,128]{2,1,0:T(1,128)S(1)}, s32[1,1,128]{2,1,0:T(1,128)}, u32[]{:S(2)}) copy-start(s32[1,1,128]{2,1,0:T(1,128)} %param.25) | copy-start | bytes 1540
  67.8 51.9 %copy-start.2 = (bf16[512,1024]{1,0:T(8,128)(2,1)S(1)}, bf16[512,1024]{1,0:T(8,128)(2,1)}, u32[]{:S(2)}) copy-start(bf16[512,1024]{1,0:T(8,128)(2,1)} %param.14) | copy-start | bytes 3145732
  67.8 54.4 %copy-start.3 = (f32[1024]{0:T(1024)S(1)}, f32[1024]{0:T(1024)}, u32[]{:S(2)}) copy-start(f32[1024]{0:T(1024)} %param.19) | copy-start | bytes 12292
  67.8 54.4 %copy-start.4 = (f32[1024]{0:T(1024)S(1)}, f32[1024]{0:T(1024)}, u32[]{:S(2)}) copy-start(f32[1024]{0:T(1024)} %param.18) | copy-start | bytes 12292
  67.8 95.4 %all-gather.16.cloned.1.call-start = ((), (), s32[]{:S(2)}) async-start(), calls=%async_computation.8 | async-start | bytes 3145728 | tf_op jit(solution)/shard_map/all_gather | solution.py:35
  78.0 88.5 %all-gather.20.cloned.1.call-start = ((), (), s32[]{:S(2)}) async-start(), calls=%async_computation.10 | async-start | bytes 3145728 | tf_op jit(solution)/shard_map/all_gather | solution.py:35
  119.6 76.6 %all-gather.12.cloned.1.call-start = ((), (), s32[]{:S(2)}) async-start(), calls=%async_computation.5 | async-start | bytes 1310720 | tf_op jit(solution)/shard_map/all_gather | solution.py:104
  162.9 80.9 %reduce-scatter.5.cloned.1.call-start = ((), (), s32[]{:S(2)}) async-start(), calls=%async_computation.6 | async-start | bytes 2621440 | tf_op jit(solution)/shard_map/reduce_scatter | solution.py:110
  206.4 0.7 copy-start.9
  206.6 37.3 %copy-start.1 = (bf16[8,16,1024]{2,1,0:T(8,128)(2,1)S(1)}, bf16[8,16,1024]{2,1,0:T(8,128)(2,1)}, u32[]{:S(2)}) copy-start(bf16[8,16,1024]{2,1,0:T(8,128)(2,1)} %copy.43) | copy-start | bytes 786436
  207.2 39.1 %copy-start.5 = (f32[1024]{0:T(1024)S(1)}, f32[1024]{0:T(1024)}, u32[]{:S(2)}) copy-start(f32[1024]{0:T(1024)} %param.23) | copy-start | bytes 12292
  207.2 39.1 %copy-start.6 = (f32[1024]{0:T(1024)S(1)}, f32[1024]{0:T(1024)}, u32[]{:S(2)}) copy-start(f32[1024]{0:T(1024)} %param.22) | copy-start | bytes 12292
Sparse Core Ops, SparseCore 0:
  31.2 46.7 all-gather.13
  80.0 39.5 all-gather.17
  121.7 22.7 all-gather.15
  146.4 20.0 all-gather.19
  169.0 27.1 all-gather.11
Sparse Core Ops, SparseCore 1:
  67.9 44.0 reduce-scatter.2
  206.5 37.3 reduce-scatter.4
where the time goes:
time: 256 us; the launch traced here: 255 us
  waiting for transfers between devices  113 us (44%)
  blocking collectives  87.8 us (34%)
  matrix products  18.1 us (7%)
  between operations  15.5 us (6%)
  local copies, waits for them, and re-layouts  10.6 us (4%)
  other arithmetic  9.59 us (4%)
    all_gather x2, waiting for transfers between devices, gather_rows(): b = lax.all_gather(a, second, axis=0, tiled=False)  51.6 us
    all_gather x2, blocking collectives, gather_rows(): a = lax.all_gather(block, first, axis=0, tiled=False)  50 us
    reduce_scatter x1, waiting for transfers between devices, local(): lax.psum_scatter(lowered_all, 'grp', scatter_dimension=0, tiled=True)  34.7 us
    all_gather x1, waiting for transfers between devices, local(): group_rows = lax.all_gather(even_rows, 'grp', axis=0, tiled=True)  26.6 us
    all_to_all x1, blocking collectives, local(): lax.all_to_all(staged, ('ry', 'rc'), split_axis=1, concat_axis=1, tiled=T...  21.8 us
    all_to_all x1, blocking collectives, local(): lax.all_to_all(staged, 'rz', split_axis=0, concat_axis=0, tiled=True)  16 us
    dot_general x1, matrix products, local(): lax.dot_general(activated, down_full_t, (((1,), (1,)), ((), ())), preferr...  10.1 us
  transfers between devices with their start and end apart: 7, of which 5 were waited for; matrix products, arithmetic and copies ran while one was open for 9% of the time, Pallas kernels for 0%

commit v1 on v0

--- a/solution.py
+++ b/solution.py
@@ -5,6 +5,7 @@
 from jax import lax
 from jax.sharding import Mesh
 from jax.sharding import PartitionSpec as P
+from jax.lax import all_to_all, axis_size
 
 EPSILON = 1e-05
 REQ = ("rz", "ry", "rc")
@@ -101,7 +102,9 @@
     staged = lax.all_to_all(staged, "rz", split_axis=0, concat_axis=0, tiled=True)
     staged = lax.all_to_all(staged, ("ry", "rc"), split_axis=1, concat_axis=1, tiled=True)
     even_rows = staged.reshape(quarter, width)
-    group_rows = lax.all_gather(even_rows, "grp", axis=0, tiled=True)
+    group_rows = jnp.concatenate(
+        all_to_all(jnp.stack([even_rows] * axis_size("grp")), "grp", 0, 0), 0
+    )
     raised = jnp.dot(group_rows, up_full, preferred_element_type=jnp.float32)
     activated = jax.nn.gelu(raised, approximate=False).astype(jnp.bfloat16)
     lowered_all = lax.dot_general(

time: 256 us -> 230 us (0.90)
  waiting for transfers between devices: 113 us -> 82.6 us
  starting transfers between devices: 0.46 us -> 4.69 us
    all_gather x1 -> x0, waiting for transfers between devices: 26.6 us -> none  [local(): group_rows = lax.all_gather(even_rows, 'grp', axis=0, tiled=True)]
    reduce_scatter x1, waiting for transfers between devices: 34.7 us -> 21.9 us  [local(): lax.psum_scatter(lowered_all, 'grp', scatter_dimension=0, tiled=True)]
    all_to_all x0 -> x1, waiting for transfers between devices: none -> 9.02 us  [local(): all_to_all(jnp.stack([even_rows] * axis_size('grp')), 'grp', 0, 0)]
    all_to_all x0 -> x1, starting transfers between devices: none -> 4.26 us  [local(): all_to_all(jnp.stack([even_rows] * axis_size('grp')), 'grp', 0, 0)]
  transfers between devices with their start and end apart: 7 -> 7, of which waited for: 5 -> 4; matrix products, arithmetic and copies ran while one was open for 9% -> 10% of each run, Pallas kernels for 0% -> 0%
where the time goes in v1:
time: 230 us; the launch traced here: 229 us
  blocking collectives  87.8 us (38%)
  waiting for transfers between devices  82.6 us (36%)
  matrix products  18.1 us (8%)
  between operations  15.5 us (7%)
  local copies, waits for them, and re-layouts  11 us (5%)
  other arithmetic  9.59 us (4%)
  starting transfers between devices  4.69 us (2%)
    all_gather x2, waiting for transfers between devices, gather_rows(): b = lax.all_gather(a, second, axis=0, tiled=False)  51.6 us
    all_gather x2, blocking collectives, gather_rows(): a = lax.all_gather(block, first, axis=0, tiled=False)  50 us
    reduce_scatter x1, waiting for transfers between devices, local(): lax.psum_scatter(lowered_all, 'grp', scatter_dimension=0, tiled=True)  21.9 us
    all_to_all x1, blocking collectives, local(): lax.all_to_all(staged, ('ry', 'rc'), split_axis=1, concat_axis=1, tiled=T...  21.8 us
    all_to_all x1, blocking collectives, local(): lax.all_to_all(staged, 'rz', split_axis=0, concat_axis=0, tiled=True)  16 us
    dot_general x1, matrix products, local(): lax.dot_general(activated, down_full_t, (((1,), (1,)), ((), ())), preferr...  10.1 us
    all_to_all x1, waiting for transfers between devices, local(): all_to_all(jnp.stack([even_rows] * axis_size('grp')), 'grp', 0, 0)  9.02 us
  transfers between devices with their start and end apart: 7, of which 4 were waited for; matrix products, arithmetic and copies ran while one was open for 10% of the time, Pallas kernels for 0%

profile of v1, /device:TPU:1, one launch (start us, length us, event | category | flops | bytes accessed | tf_op | source)
XLA Modules:
  0.0 229.3 jit_solution(2332186780631335022)
XLA Ops:
  8.1 23.0 %all-gather = bf16[64,1024]{1,0:T(8,128)(2,1)} all-gather(bf16[8,1024]{1,0:T(8,128)(2,1)} %param.20), channel_id=2, replica_groups=mesh['rz'=8,'ry'=8,'rc'=2,'grp'=4] {'ry'}, dimensions={0}, use_global_device_ids=true | all-gather | bytes 147456 | tf_op jit(solution)/shard_map/all_gather | solution.py:34
  31.1 27.1 %all-gather.3 = bf16[64,1024]{1,0:T(8,128)(2,1)} all-gather(bf16[8,1024]{1,0:T(8,128)(2,1)} %bitcast.91), channel_id=5, replica_groups=mesh['rz'=8,'ry'=8,'rc'=2,'grp'=4] {'rz'}, dimensions={0}, use_global_device_ids=true | all-gather | bytes 147456 | tf_op jit(solution)/shard_map/all_gather | solution.py:34
  58.3 2.2 fusion.101
  60.7 0.5 copy-done.6
  61.2 3.7 %while.11 = (s32[]{:T(128)}, bf16[4,512,64]{1,2,0:T(8,128)(2,1)S(1)}, bf16[4,512,64]{1,2,0:T(8,128)(2,1)S(1)}, bf16[4,512,64]{1,2,0:T(8,128)(2,1)S(1)}, bf16[4,5...) while((s32[]{:T(128)}, bf16[4,512,64]{1,2,0:T(8,128)(2,1)S(1)}, ...), condition=%wide.region_3.4_spmd.clone, body=%wide.region_0.3_spmd.clone.sunk | while | flops 70024192 | bytes 3424341 | solution.py:91
  61.2 0.4 fusion.113
  62.1 0.4 fusion.113
  62.7 0.3 fusion.115
  63.1 0.4 fusion.113
  63.7 0.3 fusion.115
  64.0 0.4 fusion.113
  64.9 2.9 %convolution_bitcast_fusion = f32[512,1024]{1,0:T(8,128)} fusion(bf16[4,64,1024]{2,1,0:T(8,128)(2,1)} %param.17, bf16[4,512,64]{1,2,0:T(8,128)(2,1)S(1)} %get-tuple-element.34), kind=kOutput, calls=%fused_computation.40 | convolution fusion | flops 268435456 | bytes 2883584 | tf_op jit(solution)/shard_map/nhd,hde->ne/dot_general | solution.py:94
  67.9 10.0 %all-gather.11.cloned.1.call-done = bf16[64,8,1024]{2,1,0:T(8,128)(2,1)} async-done(((bf16[8,8,1024]{2,1,0:T(8,128)(2,1)}), bf16[64,8,1024]{2,1,0:T(8,128)(2,1)}) %all-gather.11.cloned.1.call-update) | async-done | bytes 1048592 | tf_op jit(solution)/shard_map/all_gather | solution.py:35
  78.0 41.6 %all-gather.15.cloned.1.call-done = bf16[64,8,1024]{2,1,0:T(8,128)(2,1)} async-done(((bf16[8,8,1024]{2,1,0:T(8,128)(2,1)}), bf16[64,8,1024]{2,1,0:T(8,128)(2,1)}) %all-gather.15.cloned.1.call-update) | async-done | bytes 1048592 | tf_op jit(solution)/shard_map/all_gather | solution.py:35
  119.7 1.2 fusion.64
  120.9 1.2 multiply_reduce_fusion.1
  122.1 1.9 scatter_custom_fusion
  124.0 16.0 %all_to_all.15 = bf16[8,16,1024]{2,1,0:T(8,128)(2,1)S(1)} all-to-all(bf16[8,16,1024]{2,1,0:T(8,128)(2,1)S(1)} %bitcast.88), channel_id=1, replica_groups=mesh['rz'=8,'ry'=8,'rc'=2,'grp'=4] {'rz'}, dimensions={0} | all-to-all | bytes 524288 | tf_op jit(solution)/shard_map/all_to_all | solution.py:102
  140.2 21.8 %all_to_all.16 = bf16[8,16,1024]{2,0,1:T(8,128)(2,1)S(1)} all-to-all(bf16[8,16,1024]{2,0,1:T(8,128)(2,1)S(1)} %copy.42), channel_id=1, replica_groups=mesh['rz'=8,'ry'=8,'rc'=2,'grp'=4] {'ry','rc'}, dimensions={1} | all-to-all | bytes 524288 | tf_op jit(solution)/shard_map/all_to_all | solution.py:103
  162.1 1.1 stack.3
  163.2 4.3 %all-to-all-start.2 = ((bf16[4,128,1024]{2,1,0:T(8,128)(2,1)}), bf16[4,128,1024]{2,1,0:T(8,128)(2,1)}, u32[]{:S(2)}, u32[]{:S(2)}) async-start(bf16[4,128,1024]{2,1,0:T(8,128)(2,1)} %stack.3), calls=%async_computation.3 | async-start | bytes 2097152 | tf_op jit(solution)/shard_map/all_to_all | solution.py:106
  167.8 3.2 %copy.44 = bf16[8,8,2,8,1024]{4,3,2,1,0:T(8,128)(2,1)} copy(bf16[8,8,2,8,1024]{4,3,1,0,2:T(8,128)(2,1)} %bitcast.81) | data formatting | bytes 4194304 | tf_op jit(solution)/shard_map/transpose | solution.py:38
  170.9 3.1 %copy.45 = bf16[8,8,2,8,1024]{4,3,2,1,0:T(8,128)(2,1)} copy(bf16[8,8,2,8,1024]{4,3,0,1,2:T(8,128)(2,1)} %bitcast.82) | data formatting | bytes 4194304 | tf_op jit(solution)/shard_map/transpose | solution.py:40
  174.1 9.0 %all-to-all-done.2 = bf16[4,128,1024]{2,1,0:T(8,128)(2,1)} async-done(((bf16[4,128,1024]{2,1,0:T(8,128)(2,1)}), bf16[4,128,1024]{2,1,0:T(8,128)(2,1)}, u32[]{:S(2)}, u32[]{:S(2)}) %all-to-all-start.2) | async-done | bytes 1048608 | tf_op jit(solution)/shard_map/all_to_all | solution.py:106
  183.1 10.1 %fusion.25 = f32[512,1024]{1,0:T(8,128)} fusion(bf16[1024,1024]{1,0:T(8,128)(2,1)} %bitcast.84, bf16[512,1024]{1,0:T(8,128)(2,1)} %bitcast.12, bf16[1024,1024]{1,0:T(8,128)(2,1)} %bitcast.83), kind=kOutput, calls=%fused_computation.41 | convolution fusion | flops 2181562368 | bytes 7340032 | tf_op jit(solution)/shard_map/dot_general | solution.py:110
  193.4 0.4 copy.46
  194.0 0.8 scatter_fusion
  194.8 1.2 copy.47
  196.0 21.9 %reduce-scatter.5.cloned.1.call-done = f32[128,1024]{1,0:T(8,128)} async-done(((f32[512,1024]{1,0:T(8,128)}), f32[128,1024]{1,0:T(8,128)}) %reduce-scatter.5.cloned.1.call-update) | async-done | bytes 524304 | tf_op jit(solution)/shard_map/reduce_scatter | solution.py:113
  217.8 1.2 fusion.63
  219.0 1.2 multiply_reduce_fusion
  220.3 1.9 add_convert_fusion
  (52 shorter events, 2.9 us)
Async XLA Ops:
  8.0 50.3 %copy-start = (bf16[1024,4,192]{0,2,1:T(8,128)(2,1)S(1)}, bf16[1024,4,192]{0,2,1:T(8,128)(2,1)}, u32[]{:S(2)}) copy-start(bf16[1024,4,192]{0,2,1:T(8,128)(2,1)} %param.16) | copy-start | bytes 4718596
  8.0 69.9 %all-gather.11.cloned.1.call-start = ((), (), s32[]{:S(2)}) async-start(), calls=%async_computation.7 | async-start | bytes 1179648 | tf_op jit(solution)/shard_map/all_gather | solution.py:35
  31.1 88.5 %all-gather.15.cloned.1.call-start = ((), (), s32[]{:S(2)}) async-start(), calls=%async_computation.9 | async-start | bytes 1179648 | tf_op jit(solution)/shard_map/all_gather | solution.py:35
  58.2 61.5 %reduce-scatter.3.cloned.1.call-start = ((), (), s32[]{:S(2)}) async-start(), calls=%async_computation.5 | async-start | bytes 2621440 | tf_op jit(solution)/shard_map/reduce_scatter | solution.py:97
  60.5 0.7 copy-start.6
  67.8 10.2 %copy-start.7 = (s32[1,1,128]{2,1,0:T(1,128)S(1)}, s32[1,1,128]{2,1,0:T(1,128)}, u32[]{:S(2)}) copy-start(s32[1,1,128]{2,1,0:T(1,128)} %param.25) | copy-start | bytes 1540
  67.8 51.9 %copy-start.1 = (bf16[512,1024]{1,0:T(8,128)(2,1)S(1)}, bf16[512,1024]{1,0:T(8,128)(2,1)}, u32[]{:S(2)}) copy-start(bf16[512,1024]{1,0:T(8,128)(2,1)} %param.14) | copy-start | bytes 3145732
  67.8 54.3 %copy-start.2 = (f32[1024]{0:T(1024)S(1)}, f32[1024]{0:T(1024)}, u32[]{:S(2)}) copy-start(f32[1024]{0:T(1024)} %param.19) | copy-start | bytes 12292
  67.8 54.3 %copy-start.3 = (f32[1024]{0:T(1024)S(1)}, f32[1024]{0:T(1024)}, u32[]{:S(2)}) copy-start(f32[1024]{0:T(1024)} %param.18) | copy-start | bytes 12292
  67.8 99.9 %all-gather.13.cloned.1.call-start = ((), (), s32[]{:S(2)}) async-start(), calls=%async_computation.8 | async-start | bytes 3145728 | tf_op jit(solution)/shard_map/all_gather | solution.py:36
  78.0 93.0 %all-gather.17.cloned.1.call-start = ((), (), s32[]{:S(2)}) async-start(), calls=%async_computation.10 | async-start | bytes 3145728 | tf_op jit(solution)/shard_map/all_gather | solution.py:36
  163.2 19.9 %all-to-all-start.2 = ((bf16[4,128,1024]{2,1,0:T(8,128)(2,1)}), bf16[4,128,1024]{2,1,0:T(8,128)(2,1)}, u32[]{:S(2)}, u32[]{:S(2)}) async-start(bf16[4,128,1024]{2,1,0:T(8,128)(2,1)} %stack.3), calls=%async_computation.3 | async-start | bytes 2097152 | tf_op jit(solution)/shard_map/all_to_all | solution.py:106
  167.5 50.3 %reduce-scatter.5.cloned.1.call-start = ((), (), s32[]{:S(2)}) async-start(), calls=%async_computation.6 | async-start | bytes 2621440 | tf_op jit(solution)/shard_map/reduce_scatter | solution.py:113
  193.2 0.7 copy-start.8
  194.0 26.3 %copy-start.4 = (f32[1024]{0:T(1024)S(1)}, f32[1024]{0:T(1024)}, u32[]{:S(2)}) copy-start(f32[1024]{0:T(1024)} %param.23) | copy-start | bytes 12292
  194.0 26.3 %copy-start.5 = (f32[1024]{0:T(1024)S(1)}, f32[1024]{0:T(1024)}, u32[]{:S(2)}) copy-start(f32[1024]{0:T(1024)} %param.22) | copy-start | bytes 12292
Sparse Core Ops, SparseCore 0:
  31.2 46.7 all-gather.10
  80.0 39.5 all-gather.14
  121.7 22.7 all-gather.12
  146.4 20.0 all-gather.16
Sparse Core Ops, SparseCore 1:
  67.9 44.0 reduce-scatter.2
  193.3 24.5 reduce-scatter.4
